TPU v7x, 512 devices: a whole 4x4x16 slice. The times are simulated.
512 devices in a mesh: pipe: 4 (over y), expert: 32 (over z, core), tensor: 4 (over x).
Axes of the slice: x: 4, y: 4, z: 16, core: 2. Of those that a mesh axis runs over, the one named last changes fastest.
Arguments:
- tokens: bfloat16 [512, 6144], P('expert', ('pipe', 'tensor')), may hold values from -6 to 6
- expert_ids: int32 [512, 2], P('expert'), may hold values from 0 to 7, all different within a row; in each aligned block of 16 rows (0 to 15, 16 to 31, ...) at most 5 rows name the same one
- gates: float32 [512, 2], P('expert'), may hold values from 0.2 to 1
- w_gate: bfloat16 [32, 6144, 2048], P('expert', None, ('pipe', 'tensor')), may hold values from -0.078125 to 0.078125
- w_up: bfloat16 [32, 6144, 2048], P('expert', None, ('pipe', 'tensor')), may hold values from -0.078125 to 0.078125
- w_down: bfloat16 [32, 2048, 6144], P('expert', ('pipe', 'tensor')), may hold values from -0.0625 to 0.0625
- d_out: bfloat16 [512, 6144], P('expert', ('pipe', 'tensor')), may hold values from -6 to 6
Outputs:
- moe_out: bfloat16 [512, 6144], P('expert', ('pipe', 'tensor'))
- grad_tokens: bfloat16 [512, 6144], P('expert', ('pipe', 'tensor'))
- grad_gates: float32 [512, 2], P('expert')
Inputs may be any that keep to these rules, and one draw needn't show every extreme that they name: `expert_ids`: each row names 2 different experts. Among the rows of one index of expert (aligned blocks of 16 rows) no expert is named more than 5 times, a bound that some block reaches.
All inputs are finite; a program needn't handle non-finite values.
Results may differ from a plain program's by a relative error of at most 0.017.
Values may be sent and summed in bfloat16 or wider, within the bound.
No kernel may reach another device: no remote copies, remote signals or barrier semaphores. Data moves between devices by JAX's collectives and lax.ppermute only.
A program may use at most 64 MiB of HBM per device.

v0:
```python
import jax
import jax.numpy as jnp
from jax import lax
from jax.sharding import PartitionSpec as P


def per_device(tokens, expert_ids, gates, w_gate, w_up, w_down, d_out):
    tok_rows = tokens.shape[0]
    feat = tokens.shape[1]
    top = expert_ids.shape[1]
    devices_all = lax.axis_size("expert")
    experts = min(8, devices_all)
    group = devices_all // experts
    capacity = min(
        tok_rows,
        max(2, max(5 * tok_rows * top // (4 * experts), (tok_rows * top + experts - 1) // experts)),
    )
    slots = experts * capacity
    flat_ids = expert_ids.reshape(-1)
    onehot = (flat_ids[:, None] == jnp.arange(experts, dtype=jnp.int32)[None, :]).astype(jnp.int32)
    position = jnp.sum(jnp.cumsum(onehot, axis=0) * onehot, axis=1) - 1
    slot_of = flat_ids * capacity + position
    picks = (jnp.arange(slots, dtype=jnp.int32)[:, None] == slot_of[None, :]).astype(jnp.float32)
    pick_rows = picks.reshape(slots, tok_rows, top)
    select_tok = jnp.sum(pick_rows, axis=2).astype(jnp.bfloat16)
    select_gate = jnp.sum(pick_rows * gates[None, :, :], axis=2)
    picked = jnp.dot(select_tok, tokens, preferred_element_type=jnp.float32).astype(jnp.bfloat16)
    scaled = jnp.dot(
        select_gate, d_out.astype(jnp.float32), precision=lax.Precision.HIGHEST
    ).astype(jnp.bfloat16)
    send = jnp.concatenate([picked, scaled], axis=1).reshape(experts, capacity, 2 * feat)
    send = jnp.repeat(send, group, axis=0)
    recv = lax.all_to_all(send, "expert", split_axis=0, concat_axis=0, tiled=True)
    recv = recv.reshape(devices_all * capacity, 2 * feat)
    part_x = recv[:, :feat]
    part_dy = recv[:, feat:]
    rows_x = lax.all_gather(part_x, ("pipe", "tensor"), axis=1, tiled=True)
    rows_dy = lax.all_gather(part_dy, ("pipe", "tensor"), axis=1, tiled=True)
    gate_proj = w_gate[0]
    up_proj = w_up[0]
    down_proj = w_down[0]
    contract_last = (((1,), (1,)), ((), ()))
    h_gate = jnp.dot(rows_x, gate_proj, preferred_element_type=jnp.float32)
    h_up = jnp.dot(rows_x, up_proj, preferred_element_type=jnp.float32)
    sig = jax.nn.sigmoid(h_gate)
    hidden = (h_gate * sig * h_up).astype(jnp.bfloat16)
    out_terms = jnp.dot(hidden, down_proj, preferred_element_type=jnp.float32)
    d_hidden = lax.dot_general(
        rows_dy, down_proj, contract_last, preferred_element_type=jnp.float32
    )
    d_gate_h = (d_hidden * h_up * sig * (1.0 + h_gate * (1.0 - sig))).astype(jnp.bfloat16)
    d_up_h = (d_hidden * h_gate * sig).astype(jnp.bfloat16)
    dx_terms = lax.dot_general(
        d_gate_h, gate_proj, contract_last, preferred_element_type=jnp.float32
    )
    dx_terms = dx_terms + lax.dot_general(
        d_up_h, up_proj, contract_last, preferred_element_type=jnp.float32
    )
    out_share = lax.psum_scatter(
        out_terms.astype(jnp.bfloat16), ("pipe", "tensor"), scatter_dimension=1, tiled=True
    )
    dx_share = lax.psum_scatter(
        dx_terms.astype(jnp.bfloat16), ("pipe", "tensor"), scatter_dimension=1, tiled=True
    )
    back_send = jnp.concatenate([out_share, dx_share], axis=1).reshape(
        devices_all, capacity, 2 * feat
    )
    back = lax.all_to_all(back_send, "expert", split_axis=0, concat_axis=0, tiled=True)
    back_rows = (
        jnp.sum(back.astype(jnp.float32).reshape(experts, group, capacity, 2 * feat), axis=1)
        .astype(jnp.bfloat16)
        .reshape(slots, 2 * feat)
    )
    assign = picks.T.astype(jnp.bfloat16)
    a_both = jnp.dot(assign, back_rows, preferred_element_type=jnp.float32)
    a_out = a_both[:, :feat].reshape(tok_rows, top, feat)
    a_dx = a_both[:, feat:].reshape(tok_rows, top, feat)
    moe_out = jnp.sum(gates[:, :, None] * a_out, axis=1).astype(jnp.bfloat16)
    grad_tokens = jnp.sum(a_dx, axis=1).astype(jnp.bfloat16)
    partial_dots = jnp.sum(d_out.astype(jnp.float32)[:, None, :] * a_out, axis=2)
    grad_gates = lax.psum(partial_dots, ("pipe", "tensor"))
    return (moe_out, grad_tokens, grad_gates)


def solution(mesh):
    return jax.shard_map(
        per_device,
        mesh=mesh,
        in_specs=(
            P("expert", ("pipe", "tensor")),
            P("expert", None),
            P("expert", None),
            P("expert", None, ("pipe", "tensor")),
            P("expert", None, ("pipe", "tensor")),
            P("expert", ("pipe", "tensor"), None),
            P("expert", ("pipe", "tensor")),
        ),
        out_specs=(
            P("expert", ("pipe", "tensor")),
            P("expert", ("pipe", "tensor")),
            P("expert", None),
        ),
        check_vma=False,
    )
```

profile of v0, /device:TPU:32, one launch (start us, length us, event | category | flops | bytes accessed | tf_op | source)
XLA Modules:
  0.0 457.4 jit_solution(14242704866884179317)
XLA Ops:
  7.2 0.0 copy-start
  7.2 0.0 all-gather.3.cloned.1.call-start
  7.2 0.9 copy.35
  8.1 0.1 reshape.63
  8.2 0.1 fusion.14
  8.3 0.1 reduce_window_sum.11
  8.3 0.2 select_reduce_fusion.1
  8.5 0.1 sub.10
  8.6 0.1 copy.36
  8.7 0.7 multiply_add_fusion
  9.4 0.8 convert_reduce_fusion
  10.1 0.9 convolution_convert_fusion.1
  11.1 0.9 convolution_convert_fusion.2
  12.1 41.8 %all_to_all.10 = bf16[32,5,768]{2,1,0:T(8,128)(2,1)S(1)} all-to-all(bf16[32,5,768]{2,1,0:T(8,128)(2,1)S(1)} %bitcast.32), channel_id=1, replica_groups=mesh['pipe'=4,'expert'=32,'tensor'=4] {'expert'}, dimensions={0} | all-to-all | bytes 491520 | tf_op jit(solution)/shard_map/all_to_all | solution.py:33
  53.9 0.1 reshape.66
  54.0 0.7 fusion.21
  54.7 0.0 all-gather.3.cloned.1.call-update
  54.8 0.0 all-gather.5.cloned.1.call-start
  54.8 0.7 all-gather.5.cloned.1.call-update
  55.5 0.0 reduce-scatter.9.cloned.1.call-start
  55.6 54.5 %all-gather.3.cloned.1.call-done = bf16[160,6144]{1,0:T(8,128)(2,1)} async-done(((bf16[160,384]{1,0:T(8,128)(2,1)}), bf16[160,6144]{1,0:T(8,128)(2,1)}) %all-gather.3.cloned.1.call-update) | async-done | bytes 1966096 | tf_op jit(solution)/shard_map/all_gather | solution.py:37
  110.0 0.0 copy-done
  110.0 0.0 copy-start.1
  110.0 2.3 fusion.9
  112.4 0.0 copy-done.1
  112.4 0.0 copy-start.4
  112.4 0.0 copy-start.2
  112.4 2.2 fusion.5
  114.6 0.0 copy-start.5
  114.6 60.3 %all-gather.5.cloned.1.call-done = bf16[160,6144]{1,0:T(8,128)(2,1)} async-done(((bf16[160,384]{1,0:T(8,128)(2,1)}), bf16[160,6144]{1,0:T(8,128)(2,1)}) %all-gather.5.cloned.1.call-update) | async-done | bytes 1966096 | tf_op jit(solution)/shard_map/all_gather | solution.py:38
  174.9 0.0 copy-done.2
  174.9 2.2 fusion.1
  177.1 0.0 copy-done.4
  177.1 0.0 copy-done.5
  177.1 0.0 copy-start.3
  177.1 0.7 fusion.7
  177.8 0.7 copy-done.3
  178.5 1.6 fusion
  180.1 2.8 copy.40
  182.9 0.0 reduce-scatter.9.cloned.1.call-update
  182.9 0.0 reduce-scatter.7.cloned.1.call-start
  182.9 2.2 convolution_convert_fusion
  185.1 2.8 copy.38
  187.9 0.0 reduce-scatter.7.cloned.1.call-update
  187.9 0.0 copy-start.7
  187.9 0.0 copy-start.6
  187.9 85.6 %reduce-scatter.9.cloned.1.call-done = bf16[384,160]{1,0:T(8,128)(2,1)} async-done(((bf16[6144,160]{1,0:T(8,128)(2,1)}), bf16[384,160]{1,0:T(8,128)(2,1)}) %reduce-scatter.9.cloned.1.call-update) | async-done | bytes 122896
  273.6 1.1 copy.41
  274.6 93.5 %reduce-scatter.7.cloned.1.call-done = bf16[384,160]{1,0:T(8,128)(2,1)} async-done(((bf16[6144,160]{1,0:T(8,128)(2,1)}), bf16[384,160]{1,0:T(8,128)(2,1)}) %reduce-scatter.7.cloned.1.call-update) | async-done | bytes 122896
  368.1 1.1 copy.39
  369.2 0.8 reshape.67
  370.1 12.8 %all-to-all-start.1 = ((bf16[32,5,768]{2,1,0:T(8,128)(2,1)}), bf16[32,5,768]{2,1,0:T(8,128)(2,1)S(1)}, u32[]{:S(2)}, u32[]{:S(2)}) async-start(bf16[32,5,768]{2,1,0:T(8,128)(2,1)} %reshape.67), calls=%async_computation.1 | async-start | bytes 786432 | tf_op jit(solution)/shard_map/all_to_all | solution.py:68
  382.9 0.0 copy-done.7
  382.9 0.1 copy.34
  383.0 0.0 copy-done.6
  383.0 26.5 %all-to-all-done.1 = bf16[32,5,768]{2,1,0:T(8,128)(2,1)S(1)} async-done(((bf16[32,5,768]{2,1,0:T(8,128)(2,1)}), bf16[32,5,768]{2,1,0:T(8,128)(2,1)S(1)}, u32[]{:S(2)}, u32[]{:S(2)}) %all-to-all-start.1) | async-done | bytes 245792 | tf_op jit(solution)/shard_map/all_to_all | solution.py:68
  409.6 0.1 bitcast_reduce_fusion
  409.7 0.2 fusion.15
  409.9 0.1 multiply_reduce_fusion
  410.1 0.1 reduce_sum.72
  410.2 38.6 %psum.7 = f32[16,2]{1,0:T(8,128)S(1)} all-reduce(f32[16,2]{1,0:T(8,128)S(1)} %reduce_sum.72), channel_id=1, replica_groups=mesh['pipe'=4,'expert'=32,'tensor'=4] {'pipe','tensor'}, use_global_device_ids=true, to_apply=%region_10.11 | all-reduce | flops 32 | bytes 256 | tf_op jit(solution)/shard_map/psum | solution.py:81
  448.8 0.6 copy.37
  449.5 0.7 multiply_reduce_fusion.1
  450.2 0.7 reduce_sum.70
  (10 shorter events, 0.2 us)
Async XLA Ops:
  7.2 102.9 %copy-start = (bf16[1,6144,128]{2,1,0:T(8,128)(2,1)S(1)}, bf16[1,6144,128]{2,1,0:T(8,128)(2,1)}, u32[]{:S(2)}) copy-start(bf16[1,6144,128]{2,1,0:T(8,128)(2,1)} %param.10) | copy-start | bytes 4718596
  7.2 102.8 %all-gather.3.cloned.1.call-start = ((), (), s32[]{:S(2)}) async-start(), calls=%async_computation.4 | async-start | bytes 2088960 | tf_op jit(solution)/shard_map/all_gather | solution.py:37
  54.8 120.1 %all-gather.5.cloned.1.call-start = ((), (), s32[]{:S(2)}) async-start(), calls=%async_computation.5 | async-start | bytes 2088960 | tf_op jit(solution)/shard_map/all_gather | solution.py:38
  55.5 218.1 %reduce-scatter.9.cloned.1.call-start = ((), (), s32[]{:S(2)}) async-start(), calls=%async_computation.7 | async-start | bytes 3342336
  110.0 2.4 copy-start.1
  112.4 64.7 %copy-start.4 = (f32[160,128]{1,0:T(8,128)}, f32[160,128]{1,0:T(8,128)S(1)}, u32[]{:S(2)}) copy-start(f32[160,128]{1,0:T(8,128)S(1)} %fusion.9) | copy-start | bytes 245764
  112.4 62.5 %copy-start.2 = (bf16[1,128,6144]{2,1,0:T(8,128)(2,1)S(1)}, bf16[1,128,6144]{2,1,0:T(8,128)(2,1)}, u32[]{:S(2)}) copy-start(bf16[1,128,6144]{2,1,0:T(8,128)(2,1)} %param.12) | copy-start | bytes 4718596
  114.6 62.5 %copy-start.5 = (f32[160,128]{1,0:T(8,128)}, f32[160,128]{1,0:T(8,128)S(1)}, u32[]{:S(2)}) copy-start(f32[160,128]{1,0:T(8,128)S(1)} %fusion.5) | copy-start | bytes 245764
  177.1 1.4 copy-start.3
  182.9 185.2 %reduce-scatter.7.cloned.1.call-start = ((), (), s32[]{:S(2)}) async-start(), calls=%async_computation.6 | async-start | bytes 3342336
  187.9 195.0 %copy-start.7 = (f32[16,2]{0,1:T(2,128)S(1)}, f32[16,2]{0,1:T(2,128)}, u32[]{:S(2)}) copy-start(f32[16,2]{0,1:T(2,128)} %param.9) | copy-start | bytes 388
  187.9 195.1 %copy-start.6 = (bf16[16,384]{1,0:T(8,128)(2,1)S(1)}, bf16[16,384]{1,0:T(8,128)(2,1)}, u32[]{:S(2)}) copy-start(bf16[16,384]{1,0:T(8,128)(2,1)} %param.13) | copy-start | bytes 36868
  370.1 39.5 %all-to-all-start.1 = ((bf16[32,5,768]{2,1,0:T(8,128)(2,1)}), bf16[32,5,768]{2,1,0:T(8,128)(2,1)S(1)}, u32[]{:S(2)}, u32[]{:S(2)}) async-start(bf16[32,5,768]{2,1,0:T(8,128)(2,1)} %reshape.67), calls=%async_computation.1 | async-start | bytes 786432 | tf_op jit(solution)/shard_map/all_to_all | solution.py:68
Sparse Core Ops, SparseCore 0:
  54.9 55.0 all-gather.2
  113.0 61.8 all-gather.4
  183.0 90.5 reduce-scatter.8
  277.6 90.4 reduce-scatter.6
where the time goes:
time: 458 us; the launch traced here: 457 us
  waiting for transfers between devices  321 us (70%)
  blocking collectives  80.5 us (18%)
  between operations  14 us (3%)
  matrix products  13.2 us (3%)
  starting transfers between devices  13 us (3%)
  local copies, waits for them, and re-layouts  12.2 us (3%)
    unnamed x6, waiting for transfers between devices  180 us
    all_gather x1, waiting for transfers between devices, per_device(): rows_dy = lax.all_gather(part_dy, ('pipe', 'tensor'), axis=1, tiled=True)  60.3 us
    all_gather x1, waiting for transfers between devices, per_device(): rows_x = lax.all_gather(part_x, ('pipe', 'tensor'), axis=1, tiled=True)  54.5 us
    all_to_all x1, blocking collectives, per_device(): lax.all_to_all(send, 'expert', split_axis=0, concat_axis=0, tiled=True)  41.8 us
    psum x1, blocking collectives, per_device(): grad_gates = lax.psum(partial_dots, ('pipe', 'tensor'))  38.6 us
    all_to_all x1, waiting for transfers between devices, per_device(): lax.all_to_all(back_send, 'expert', split_axis=0, concat_axis=0, tiled=True)  26.5 us
    all_to_all x1, starting transfers between devices, per_device(): lax.all_to_all(back_send, 'expert', split_axis=0, concat_axis=0, tiled=True)  12.8 us
    unnamed x23, local copies, waits for them, and re-layouts  9.97 us
  transfers between devices with their start and end apart: 5, of which 5 were waited for; matrix products, arithmetic and copies ran while one was open for 2% of the time, Pallas kernels for 0%

commit v1 on v0

--- a/solution.py
+++ b/solution.py
@@ -78,7 +78,7 @@
     moe_out = jnp.sum(gates[:, :, None] * a_out, axis=1).astype(jnp.bfloat16)
     grad_tokens = jnp.sum(a_dx, axis=1).astype(jnp.bfloat16)
     partial_dots = jnp.sum(d_out.astype(jnp.float32)[:, None, :] * a_out, axis=2)
-    grad_gates = lax.psum(partial_dots, ("pipe", "tensor"))
+    grad_gates = lax.psum(lax.psum(partial_dots, "tensor"), "pipe")
     return (moe_out, grad_tokens, grad_gates)
 
 

time: 458 us -> 440 us (0.961)
  the two profiles are of different devices: /device:TPU:32 before, /device:TPU:2 now
where the time goes in v1:
time: 440 us; the launch traced here: 439 us
  waiting for transfers between devices  321 us (73%)
  blocking collectives  62.4 us (14%)
  between operations  14 us (3%)
  matrix products  13.2 us (3%)
  starting transfers between devices  12.7 us (3%)
  local copies, waits for them, and re-layouts  12.2 us (3%)
    unnamed x6, waiting for transfers between devices  180 us
    all_gather x1, waiting for transfers between devices, per_device(): rows_dy = lax.all_gather(part_dy, ('pipe', 'tensor'), axis=1, tiled=True)  60.3 us
    all_gather x1, waiting for transfers between devices, per_device(): rows_x = lax.all_gather(part_x, ('pipe', 'tensor'), axis=1, tiled=True)  52.8 us
    all_to_all x1, blocking collectives, per_device(): lax.all_to_all(send, 'expert', split_axis=0, concat_axis=0, tiled=True)  43.5 us
    all_to_all x1, waiting for transfers between devices, per_device(): lax.all_to_all(back_send, 'expert', split_axis=0, concat_axis=0, tiled=True)  28.1 us
    psum x2, blocking collectives, per_device(): grad_gates = lax.psum(lax.psum(partial_dots, 'tensor'), 'pipe')  18.9 us
    all_to_all x1, starting transfers between devices, per_device(): lax.all_to_all(back_send, 'expert', split_axis=0, concat_axis=0, tiled=True)  12.5 us
    unnamed x23, local copies, waits for them, and re-layouts  9.97 us
  transfers between devices with their start and end apart: 5, of which 5 were waited for; matrix products, arithmetic and copies ran while one was open for 2% of the time, Pallas kernels for 0%

profile of v1, /device:TPU:2, one launch (start us, length us, event | category | flops | bytes accessed | tf_op | source)
XLA Modules:
  0.0 438.9 jit_solution(15398137807818277859)
XLA Ops:
  7.2 0.0 copy-start
  7.2 0.0 all-gather.3.cloned.1.call-start
  7.2 0.9 copy.35
  8.1 0.1 reshape.63
  8.2 0.1 fusion.14
  8.3 0.1 reduce_window_sum.11
  8.3 0.2 select_reduce_fusion.1
  8.5 0.1 sub.10
  8.6 0.1 copy.36
  8.7 0.7 multiply_add_fusion
  9.4 0.8 convert_reduce_fusion
  10.1 0.9 convolution_convert_fusion.1
  11.1 0.9 convolution_convert_fusion.2
  12.1 43.5 %all_to_all.10 = bf16[32,5,768]{2,1,0:T(8,128)(2,1)S(1)} all-to-all(bf16[32,5,768]{2,1,0:T(8,128)(2,1)S(1)} %bitcast.32), channel_id=1, replica_groups=mesh['pipe'=4,'expert'=32,'tensor'=4] {'expert'}, dimensions={0} | all-to-all | bytes 491520 | tf_op jit(solution)/shard_map/all_to_all | solution.py:33
  55.6 0.1 reshape.66
  55.7 0.7 fusion.21
  56.4 0.0 all-gather.3.cloned.1.call-update
  56.4 0.0 all-gather.5.cloned.1.call-start
  56.5 0.7 all-gather.5.cloned.1.call-update
  57.2 0.0 reduce-scatter.9.cloned.1.call-start
  57.2 52.8 %all-gather.3.cloned.1.call-done = bf16[160,6144]{1,0:T(8,128)(2,1)} async-done(((bf16[160,384]{1,0:T(8,128)(2,1)}), bf16[160,6144]{1,0:T(8,128)(2,1)}) %all-gather.3.cloned.1.call-update) | async-done | bytes 1966096 | tf_op jit(solution)/shard_map/all_gather | solution.py:37
  110.1 0.0 copy-done
  110.1 2.3 fusion.9
  112.4 0.0 copy-done.1
  112.4 0.0 copy-start.4
  112.5 0.0 copy-start.2
  112.5 2.2 fusion.5
  114.7 0.0 copy-start.5
  114.7 60.3 %all-gather.5.cloned.1.call-done = bf16[160,6144]{1,0:T(8,128)(2,1)} async-done(((bf16[160,384]{1,0:T(8,128)(2,1)}), bf16[160,6144]{1,0:T(8,128)(2,1)}) %all-gather.5.cloned.1.call-update) | async-done | bytes 1966096 | tf_op jit(solution)/shard_map/all_gather | solution.py:38
  174.9 0.0 copy-done.2
  174.9 2.2 fusion.1
  177.2 0.0 copy-done.4
  177.2 0.0 copy-done.5
  177.2 0.0 copy-start.3
  177.2 0.7 fusion.7
  177.9 0.7 copy-done.3
  178.6 1.6 fusion
  180.2 2.8 copy.40
  182.9 0.0 reduce-scatter.9.cloned.1.call-update
  182.9 0.0 reduce-scatter.7.cloned.1.call-start
  183.0 2.2 convolution_convert_fusion
  185.2 2.8 copy.38
  187.9 0.0 reduce-scatter.7.cloned.1.call-update
  188.0 0.0 copy-start.7
  188.0 0.0 copy-start.6
  188.0 85.6 %reduce-scatter.9.cloned.1.call-done = bf16[384,160]{1,0:T(8,128)(2,1)} async-done(((bf16[6144,160]{1,0:T(8,128)(2,1)}), bf16[384,160]{1,0:T(8,128)(2,1)}) %reduce-scatter.9.cloned.1.call-update) | async-done | bytes 122896
  273.6 1.1 copy.41
  274.7 93.5 %reduce-scatter.7.cloned.1.call-done = bf16[384,160]{1,0:T(8,128)(2,1)} async-done(((bf16[6144,160]{1,0:T(8,128)(2,1)}), bf16[384,160]{1,0:T(8,128)(2,1)}) %reduce-scatter.7.cloned.1.call-update) | async-done | bytes 122896
  368.1 1.1 copy.39
  369.2 0.8 reshape.67
  370.1 12.5 %all-to-all-start.1 = ((bf16[32,5,768]{2,1,0:T(8,128)(2,1)}), bf16[32,5,768]{2,1,0:T(8,128)(2,1)S(1)}, u32[]{:S(2)}, u32[]{:S(2)}) async-start(bf16[32,5,768]{2,1,0:T(8,128)(2,1)} %reshape.67), calls=%async_computation.1 | async-start | bytes 786432 | tf_op jit(solution)/shard_map/all_to_all | solution.py:68
  382.6 0.0 copy-done.7
  382.6 0.1 copy.34
  382.7 0.0 copy-done.6
  382.8 28.1 %all-to-all-done.1 = bf16[32,5,768]{2,1,0:T(8,128)(2,1)S(1)} async-done(((bf16[32,5,768]{2,1,0:T(8,128)(2,1)}), bf16[32,5,768]{2,1,0:T(8,128)(2,1)S(1)}, u32[]{:S(2)}, u32[]{:S(2)}) %all-to-all-start.1) | async-done | bytes 245792 | tf_op jit(solution)/shard_map/all_to_all | solution.py:68
  410.9 0.1 bitcast_reduce_fusion
  411.0 0.2 fusion.15
  411.2 0.1 multiply_reduce_fusion
  411.4 0.1 reduce_sum.72
  411.5 8.8 %psum.14 = f32[16,2]{1,0:T(8,128)S(1)} all-reduce(f32[16,2]{1,0:T(8,128)S(1)} %reduce_sum.72), channel_id=1, replica_groups=mesh['pipe'=4,'expert'=32,'tensor'=4] {'tensor'}, use_global_device_ids=true, to_apply=%region_10.11 | all-reduce | flops 32 | bytes 256 | tf_op jit(solution)/shard_map/psum | solution.py:81
  420.2 10.1 %psum.15 = f32[16,2]{1,0:T(8,128)S(1)} all-reduce(f32[16,2]{1,0:T(8,128)S(1)} %psum.14), channel_id=1, replica_groups=mesh['pipe'=4,'expert'=32,'tensor'=4] {'pipe'}, use_global_device_ids=true, to_apply=%region_11.12 | all-reduce | flops 32 | bytes 256 | tf_op jit(solution)/shard_map/psum | solution.py:81
  430.4 0.6 copy.37
  431.0 0.7 multiply_reduce_fusion.1
  431.7 0.7 reduce_sum.70
  (11 shorter events, 0.3 us)
Async XLA Ops:
  7.2 102.9 %copy-start = (bf16[1,6144,128]{2,1,0:T(8,128)(2,1)S(1)}, bf16[1,6144,128]{2,1,0:T(8,128)(2,1)}, u32[]{:S(2)}) copy-start(bf16[1,6144,128]{2,1,0:T(8,128)(2,1)} %param.10) | copy-start | bytes 4718596
  7.2 102.9 %all-gather.3.cloned.1.call-start = ((), (), s32[]{:S(2)}) async-start(), calls=%async_computation.4 | async-start | bytes 2088960 | tf_op jit(solution)/shard_map/all_gather | solution.py:37
  56.4 118.5 %all-gather.5.cloned.1.call-start = ((), (), s32[]{:S(2)}) async-start(), calls=%async_computation.5 | async-start | bytes 2088960 | tf_op jit(solution)/shard_map/all_gather | solution.py:38
  57.2 216.4 %reduce-scatter.9.cloned.1.call-start = ((), (), s32[]{:S(2)}) async-start(), calls=%async_computation.7 | async-start | bytes 3342336
  110.1 2.4 copy-start.1
  112.4 64.7 %copy-start.4 = (f32[160,128]{1,0:T(8,128)}, f32[160,128]{1,0:T(8,128)S(1)}, u32[]{:S(2)}) copy-start(f32[160,128]{1,0:T(8,128)S(1)} %fusion.9) | copy-start | bytes 245764
  112.5 62.5 %copy-start.2 = (bf16[1,128,6144]{2,1,0:T(8,128)(2,1)S(1)}, bf16[1,128,6144]{2,1,0:T(8,128)(2,1)}, u32[]{:S(2)}) copy-start(bf16[1,128,6144]{2,1,0:T(8,128)(2,1)} %param.12) | copy-start | bytes 4718596
  114.7 62.5 %copy-start.5 = (f32[160,128]{1,0:T(8,128)}, f32[160,128]{1,0:T(8,128)S(1)}, u32[]{:S(2)}) copy-start(f32[160,128]{1,0:T(8,128)S(1)} %fusion.5) | copy-start | bytes 245764
  177.2 1.4 copy-start.3
  182.9 185.2 %reduce-scatter.7.cloned.1.call-start = ((), (), s32[]{:S(2)}) async-start(), calls=%async_computation.6 | async-start | bytes 3342336
  188.0 194.7 %copy-start.7 = (f32[16,2]{0,1:T(2,128)S(1)}, f32[16,2]{0,1:T(2,128)}, u32[]{:S(2)}) copy-start(f32[16,2]{0,1:T(2,128)} %param.9) | copy-start | bytes 388
  188.0 194.7 %copy-start.6 = (bf16[16,384]{1,0:T(8,128)(2,1)S(1)}, bf16[16,384]{1,0:T(8,128)(2,1)}, u32[]{:S(2)}) copy-start(bf16[16,384]{1,0:T(8,128)(2,1)} %param.13) | copy-start | bytes 36868
  370.1 40.8 %all-to-all-start.1 = ((bf16[32,5,768]{2,1,0:T(8,128)(2,1)}), bf16[32,5,768]{2,1,0:T(8,128)(2,1)S(1)}, u32[]{:S(2)}, u32[]{:S(2)}) async-start(bf16[32,5,768]{2,1,0:T(8,128)(2,1)} %reshape.67), calls=%async_computation.1 | async-start | bytes 786432 | tf_op jit(solution)/shard_map/all_to_all | solution.py:68
Sparse Core Ops, SparseCore 0:
  56.6 53.4 all-gather.2
  113.1 61.8 all-gather.4
  183.1 90.4 reduce-scatter.8
  277.7 90.4 reduce-scatter.6
